TPU v7x, 512 devices: a whole 4x8x8 slice. The times are simulated.
512 devices in a mesh: pairs: 128 (over y, z, core), tensor: 4 (over x).
Axes of the slice: x: 4, y: 8, z: 8, core: 2. Of those that a mesh axis runs over, the one named last changes fastest.
Arguments:
- queries: bfloat16 [32768, 4096], P('pairs', 'tensor'), may hold values from -100 to 100
- key_rows: bfloat16 [32768, 4096], P('pairs', 'tensor'), may hold values from -3.5 to 3.5
- value_rows: bfloat16 [32768, 4096], P('pairs', 'tensor'), may hold values from -12 to 12
- pair_ids: int32 [32768], P('pairs'), may hold values from 0 to 8, as said below
- out_weight: bfloat16 [4096, 4096], P('tensor', 'pairs'), may hold values from -0.09375 to 0.09375
- residual: bfloat16 [24576, 4096], P('pairs', 'tensor'), may hold values from -6 to 6
Outputs:
- hidden_out: bfloat16 [24576, 4096], P('pairs', 'tensor')
Inputs may be any that keep to these rules, and one draw needn't show every extreme that they name: `pair_ids`: within each block of 256 rows the entries never fall; rows with a value below 8 come first and rows with value 8 form the block's tail; equal values below 8 form one pair. The used rows of blocks 2k and 2k + 1 together number at most 384, reached by some two blocks, and some block has no unused row.
All inputs are finite; a program needn't handle non-finite values.
Results may differ from a plain program's by a relative error of at most 0.0055.
Values may be sent and summed in bfloat16 or wider, within the bound.
No kernel may reach another device: no remote copies, remote signals or barrier semaphores. Data moves between devices by JAX's collectives and lax.ppermute only.
A program may use at most 64 MiB of HBM per device.

v0:
```python
import jax
import jax.numpy as jnp
from jax import lax
from jax.sharding import PartitionSpec as P

HEAD = 64
SLOTS = 8


def carried_in(part, axis, combine, identity):
    place = lax.axis_index(axis)
    gathered = lax.all_gather(part, axis)
    state = jnp.zeros_like(part) + jnp.asarray(identity, part.dtype)

    def one(step, state):
        return combine(state, lax.dynamic_index_in_dim(gathered, step, 0, False))

    return lax.fori_loop(0, place, one, state)


def attend_group(query_part, key_part, value_part, allowed):
    scores = jnp.einsum("qhd,khd->hqk", query_part, key_part, preferred_element_type=jnp.float32)
    masked = jnp.where(allowed[None], scores, -1e30)
    row_top = jnp.max(masked, axis=2, keepdims=True)
    exp_terms = jnp.where(allowed[None], jnp.exp(masked - row_top), 0.0)
    row_total = jnp.maximum(jnp.sum(exp_terms, axis=2, keepdims=True), 1.0)
    weights = (exp_terms / row_total).astype(jnp.bfloat16)
    mixed = jnp.einsum("hqk,khd->qhd", weights, value_part, preferred_element_type=jnp.float32)
    return mixed.astype(jnp.bfloat16)


def add_counts(earlier, later):
    return earlier + later


def shards(queries, key_rows, value_rows, pair_ids, out_weight, residual):
    cap_rows = queries.shape[0]
    local_width = queries.shape[1]
    heads_local = local_width // HEAD
    group_size = 4
    balanced_rows = residual.shape[0]
    allowed = (pair_ids[:, None] == pair_ids[None, :]) & (pair_ids[:, None] < SLOTS)

    def split_heads(stacked):
        return stacked.reshape(cap_rows, heads_local // group_size, group_size, HEAD).transpose(
            1, 0, 2, 3
        )

    def per_group(operands):
        return attend_group(operands[0], operands[1], operands[2], allowed)

    grouped = lax.map(
        per_group, (split_heads(queries), split_heads(key_rows), split_heads(value_rows))
    )
    attended = grouped.transpose(1, 0, 2, 3).reshape(cap_rows, local_width)
    live_rows = jnp.sum((pair_ids < SLOTS).astype(jnp.int32))
    devices = lax.axis_size("pairs")
    row_start = carried_in(live_rows.reshape(1), "pairs", add_counts, jnp.zeros((1,), jnp.int32))[0]
    partial_value = jnp.dot(
        attended,
        lax.all_gather(out_weight, "pairs", axis=1, tiled=True),
        preferred_element_type=jnp.float32,
    )
    payload = lax.psum_scatter(
        partial_value.astype(jnp.bfloat16), "tensor", scatter_dimension=1, tiled=True
    )
    per_peer = cap_rows // devices
    feature_width = payload.shape[1]
    peer_index = jnp.arange(devices, dtype=jnp.int32)
    turn_index = jnp.arange(per_peer, dtype=jnp.int32)
    source_rows = ((peer_index - row_start) % devices)[:, None] + devices * turn_index[None, :]
    slot_index = jnp.where(
        source_rows < live_rows, (row_start + source_rows) // devices, balanced_rows
    ).astype(jnp.int32)
    outgoing = jnp.take(payload, source_rows.reshape(-1), axis=0).reshape(
        devices, per_peer, feature_width
    )
    incoming = lax.all_to_all(outgoing, "pairs", split_axis=0, concat_axis=0, tiled=True)
    incoming_slots = lax.all_to_all(slot_index, "pairs", split_axis=0, concat_axis=0, tiled=True)
    landed = jnp.zeros((balanced_rows, feature_width), payload.dtype)
    moved_rows = landed.at[incoming_slots.reshape(-1)].set(
        incoming.reshape(-1, feature_width), mode="drop"
    )
    return (residual.astype(jnp.float32) + moved_rows.astype(jnp.float32)).astype(jnp.bfloat16)


def solution(mesh):
    in_specs = (
        P("pairs", "tensor"),
        P("pairs", "tensor"),
        P("pairs", "tensor"),
        P("pairs"),
        P("tensor", "pairs"),
        P("pairs", "tensor"),
    )
    out_specs = P("pairs", "tensor")
    return jax.shard_map(shards, mesh=mesh, in_specs=in_specs, out_specs=out_specs, check_vma=False)
```

profile of v0, /device:TPU:2, one launch (start us, length us, event | category | flops | bytes accessed | tf_op | source)
XLA Modules:
  0.0 358.3 jit_solution(10043255233343944418)
XLA Ops:
  6.5 0.7 all-gather.2.cloned.1.call-update
  7.3 1.2 copy.21
  8.6 1.2 copy.22
  9.8 1.2 copy.23
  11.1 1.4 convert_reduce_fusion
  12.4 9.2 %while.22 = (s32[]{:T(128)}, bf16[4,256,4,64]{1,3,2,0:T(8,128)(2,1)S(1)}, bf16[4,256,4,64]{1,3,2,0:T(8,128)(2,1)S(1)}, bf16[4,256,4,64]{1,3,2,0:T(8,128)(2,1)S(1...) while((s32[]{:T(128)}, ...), condition=%wide.region_6.7_spmd.clone, body=%wide.region_3.6_spmd.clone.sunk | while | flops 103221760 | bytes 1134941 | solution.py:52
  12.4 0.9 compare_and_fusion.3
  13.3 0.6 fusion.64
  13.9 0.8 fusion.65
  14.7 0.9 compare_and_fusion.3
  15.6 0.6 fusion.64
  16.2 0.8 fusion.65
  17.0 0.9 compare_and_fusion.3
  18.5 0.8 fusion.65
  19.4 0.9 compare_and_fusion.3
  20.2 0.6 fusion.64
  20.8 0.8 fusion.65
  21.7 81.6 %all-gather.2.cloned.1.call-done = bf16[1024,4096]{0,1:T(8,128)(2,1)} async-done(((bf16[1024,32]{0,1:T(8,128)(2,1)}), bf16[1024,4096]{0,1:T(8,128)(2,1)}) %all-gather.2.cloned.1.call-update) | async-done | bytes 8388624 | tf_op jit(solution)/shard_map/all_gather | solution.py:61
  103.3 7.2 %convolution_convert_fusion.1 = bf16[256,4096]{1,0:T(8,128)(2,1)} fusion(bf16[256,1024]{0,1:T(8,128)(2,1)S(1)} %bitcast.75, bf16[1024,4096]{0,1:T(8,128)(2,1)} %all-gather.2.cloned.1.call-done), kind=kOutput, calls=%fused_computation.29 | convolution fusion | flops 2148532224 | bytes 11010048 | tf_op jit(solution)/shard_map/dot_general | solution.py:59
  110.5 1.4 dynamic-slice
  111.9 1.4 dynamic-update-slice
  113.3 22.5 %all-reduce = s32[128]{0:T(128)S(1)} all-reduce(s32[128]{0:T(128)S(1)} %dynamic-update-slice), channel_id=1, replica_groups=mesh['pairs'=128,'tensor'=4] {'pairs'}, use_global_device_ids=true, to_apply=%add | all-reduce | flops 128 | bytes 1024
  135.9 1.7 compare_select_fusion
  137.6 171.8 %all-to-all-start = ((s32[128,1,2]{2,1,0:T(1,128)}), s32[128,1,2]{2,1,0:T(1,128)S(1)}, u32[]{:S(2)}, u32[]{:S(2)}) async-start(s32[128,1,2]{2,1,0:T(1,128)} %compare_select_fusion), calls=%async_computation | async-start | bytes 131072 | tf_op jit(solution)/shard_map/all_to_all | solution.py:79
  310.0 2.7 gather_fusion
  312.9 1.4 broadcast_select_fusion
  314.2 6.3 %all-to-all-done = s32[128,1,2]{2,1,0:T(1,128)S(1)} async-done(((s32[128,1,2]{2,1,0:T(1,128)}), s32[128,1,2]{2,1,0:T(1,128)S(1)}, u32[]{:S(2)}, u32[]{:S(2)}) %all-to-all-start) | async-done | bytes 1056 | tf_op jit(solution)/shard_map/all_to_all | solution.py:79
  320.5 7.5 %all-to-all-start.1 = ((bf16[128,2,1024]{2,1,0:T(2,128)(2,1)}), bf16[128,2,1024]{2,1,0:T(2,128)(2,1)S(1)}, u32[]{:S(2)}, u32[]{:S(2)}) async-start(bf16[128,2,1024]{2,1,0:T(2,128)(2,1)} %broadcast_select_fusion), calls=%async_computation.2 | async-start | bytes 1048576 | tf_op jit(solution)/shard_map/all_to_all | solution.py:78
  328.5 0.8 reduce.3
  329.4 19.2 %all-to-all-done.1 = bf16[128,2,1024]{2,1,0:T(2,128)(2,1)S(1)} async-done(((bf16[128,2,1024]{2,1,0:T(2,128)(2,1)}), bf16[128,2,1024]{2,1,0:T(2,128)(2,1)S(1)}, u32[]{:S(2)}, u32[]{:S(2)}) %all-to-all-start.1) | async-done | bytes 524320 | tf_op jit(solution)/shard_map/all_to_all | solution.py:78
  348.8 1.8 scatter_custom_fusion
  350.6 0.9 add_convert_fusion
  (28 shorter events, 2.3 us)
Async XLA Ops:
  6.5 96.7 %all-gather.2.cloned.1.call-start = ((), (), s32[]{:S(2)}) async-start(), calls=%async_computation.3 | async-start | bytes 8454144 | tf_op jit(solution)/shard_map/all_gather | solution.py:61
  7.3 302.7 %reduce-scatter.2.cloned.1.call-start = ((), (), s32[]{:S(2)}) async-start(), calls=%async_computation.4 | async-start | bytes 2621440 | tf_op jit(solution)/shard_map/reduce_scatter | solution.py:64
  110.5 240.1 %copy-start = (bf16[192,1024]{1,0:T(8,128)(2,1)S(1)}, bf16[192,1024]{1,0:T(8,128)(2,1)}, u32[]{:S(2)}) copy-start(bf16[192,1024]{1,0:T(8,128)(2,1)} %param.15) | copy-start | bytes 1179652
  137.6 182.9 %all-to-all-start = ((s32[128,1,2]{2,1,0:T(1,128)}), s32[128,1,2]{2,1,0:T(1,128)S(1)}, u32[]{:S(2)}, u32[]{:S(2)}) async-start(s32[128,1,2]{2,1,0:T(1,128)} %compare_select_fusion), calls=%async_computation | async-start | bytes 131072 | tf_op jit(solution)/shard_map/all_to_all | solution.py:79
  320.5 28.1 %all-to-all-start.1 = ((bf16[128,2,1024]{2,1,0:T(2,128)(2,1)}), bf16[128,2,1024]{2,1,0:T(2,128)(2,1)S(1)}, u32[]{:S(2)}, u32[]{:S(2)}) async-start(bf16[128,2,1024]{2,1,0:T(2,128)(2,1)} %broadcast_select_fusion), calls=%async_computation.2 | async-start | bytes 1048576 | tf_op jit(solution)/shard_map/all_to_all | solution.py:78
Sparse Core Ops, SparseCore 0:
  10.5 92.7 all-gather.1
  110.6 30.4 reduce-scatter.1
where the time goes:
time: 360 us; the launch traced here: 358 us
  starting transfers between devices  179 us (50%)
  waiting for transfers between devices  108 us (30%)
  blocking collectives  22.5 us (6%)
  between operations  13.5 us (4%)
  matrix products  12.9 us (4%)
  local copies, waits for them, and re-layouts  12.4 us (3%)
  other arithmetic  9.83 us (3%)
    all_to_all x1, starting transfers between devices, shards(): lax.all_to_all(slot_index, 'pairs', split_axis=0, concat_axis=0, tiled=True)  172 us
    all_gather x1, waiting for transfers between devices, shards(): lax.all_gather(out_weight, 'pairs', axis=1, tiled=True)  81.6 us
    unnamed x1, blocking collectives  22.5 us
    all_to_all x1, waiting for transfers between devices, shards(): lax.all_to_all(outgoing, 'pairs', split_axis=0, concat_axis=0, tiled=True)  19.2 us
    all_to_all x1, starting transfers between devices, shards(): lax.all_to_all(outgoing, 'pairs', split_axis=0, concat_axis=0, tiled=True)  7.48 us
    dot_general x1, matrix products, shards(): jnp.dot(attended, lax.all_gather(out_weight, 'pairs', axis=1, tiled=True)...  7.2 us
  transfers between devices with their start and end apart: 4, of which 3 were waited for; matrix products, arithmetic and copies ran while one was open for 7% of the time, Pallas kernels for 0%

commit v1 on v0

--- a/solution.py
+++ b/solution.py
@@ -1,3 +1,4 @@
+import functools
 import jax
 import jax.numpy as jnp
 from jax import lax
@@ -5,6 +6,15 @@
 
 HEAD = 64
 SLOTS = 8
+
+
+def mix_table(xin, mesh_ax):
+    return jnp.concatenate(
+        lax.all_to_all(jnp.stack(lax.axis_size(mesh_ax) * [xin]), mesh_ax, 0, 0), 1
+    )
+
+
+read_ranges_for = functools.partial(mix_table, mesh_ax="pairs")
 
 
 def carried_in(part, axis, combine, identity):
@@ -57,9 +67,7 @@
     devices = lax.axis_size("pairs")
     row_start = carried_in(live_rows.reshape(1), "pairs", add_counts, jnp.zeros((1,), jnp.int32))[0]
     partial_value = jnp.dot(
-        attended,
-        lax.all_gather(out_weight, "pairs", axis=1, tiled=True),
-        preferred_element_type=jnp.float32,
+        attended, read_ranges_for(out_weight), preferred_element_type=jnp.float32
     )
     payload = lax.psum_scatter(
         partial_value.astype(jnp.bfloat16), "tensor", scatter_dimension=1, tiled=True

time: 360 us -> 554 us (1.54)
  the two profiles are of different devices: /device:TPU:2 before, /device:TPU:6 now
where the time goes in v1:
time: 554 us; the launch traced here: 552 us
  waiting for transfers between devices  238 us (43%)
  starting transfers between devices  202 us (36%)
  blocking collectives  65.4 us (12%)
  local copies, waits for them, and re-layouts  14.3 us (3%)
  between operations  13.6 us (2%)
  matrix products  12.9 us (2%)
  other arithmetic  5.95 us (1%)
    all_to_all x1, waiting for transfers between devices, mix_table(): lax.all_to_all(jnp.stack(lax.axis_size(mesh_ax) * [xin]), mesh_ax, 0, 0)  213 us
    all_to_all x1, starting transfers between devices, shards(): lax.all_to_all(slot_index, 'pairs', split_axis=0, concat_axis=0, tiled=True)  176 us
    unnamed x1, blocking collectives  65.4 us
    all_to_all x1, waiting for transfers between devices, shards(): lax.all_to_all(outgoing, 'pairs', split_axis=0, concat_axis=0, tiled=True)  19.2 us
    all_to_all x1, starting transfers between devices, mix_table(): lax.all_to_all(jnp.stack(lax.axis_size(mesh_ax) * [xin]), mesh_ax, 0, 0)  18.5 us
  transfers between devices with their start and end apart: 4, of which 3 were waited for; matrix products, arithmetic and copies ran while one was open for 3% of the time, Pallas kernels for 0%

profile of v1, /device:TPU:6, one launch (start us, length us, event | category | flops | bytes accessed | tf_op | source)
XLA Modules:
  0.0 552.4 jit_solution(9782126384844481125)
XLA Ops:
  6.5 5.1 stack.2
  11.7 18.5 %all-to-all-start.1 = ((bf16[128,1024,32]{1,2,0:T(8,128)(2,1)}), bf16[128,1024,32]{1,2,0:T(8,128)(2,1)}, u32[]{:S(2)}, u32[]{:S(2)}) async-start(bf16[128,1024,32]{1,2,0:T(8,128)(2,1)} %stack.2), calls=%async_computation.1 | async-start | bytes 16777216 | tf_op jit(solution)/shard_map/all_to_all | solution.py:13
  30.2 0.2 copy.22
  30.4 0.2 copy.23
  30.7 0.2 copy.24
  30.9 0.6 convert_reduce_fusion
  31.5 6.2 %while.22 = (s32[]{:T(128)}, bf16[4,256,4,64]{1,3,2,0:T(8,128)(2,1)S(1)}, bf16[4,256,4,64]{1,3,2,0:T(8,128)(2,1)S(1)}, bf16[4,256,4,64]{1,3,2,0:T(8,128)(2,1)S(1...) while((s32[]{:T(128)}, ...), condition=%wide.region_6.7_spmd.clone, body=%wide.region_3.6_spmd.clone.sunk | while | flops 103221760 | bytes 1134941 | solution.py:62
  31.6 0.6 fusion.64
  32.2 0.8 fusion.65
  33.2 0.6 fusion.64
  33.8 0.8 fusion.65
  34.7 0.6 fusion.64
  35.3 0.8 fusion.65
  36.3 0.6 fusion.64
  36.9 0.8 fusion.65
  37.7 213.2 %all-to-all-done.1 = bf16[128,1024,32]{1,2,0:T(8,128)(2,1)} async-done(((bf16[128,1024,32]{1,2,0:T(8,128)(2,1)}), bf16[128,1024,32]{1,2,0:T(8,128)(2,1)}, u32[]{:S(2)}, u32[]{:S(2)}) %all-to-all-start.1) | async-done | bytes 8388640 | tf_op jit(solution)/shard_map/all_to_all | solution.py:13
  250.9 7.2 %convolution_convert_fusion.1 = bf16[256,4096]{1,0:T(8,128)(2,1)} fusion(bf16[256,1024]{0,1:T(8,128)(2,1)S(1)} %bitcast.78, bf16[1024,4096]{0,1:T(8,128)(2,1)} %bitcast.15), kind=kOutput, calls=%fused_computation.29 | convolution fusion | flops 2148532224 | bytes 11010048 | tf_op jit(solution)/shard_map/dot_general | solution.py:69
  258.1 1.4 dynamic-slice
  259.5 1.3 dynamic-update-slice
  260.9 65.4 %all-reduce = s32[128]{0:T(128)S(1)} all-reduce(s32[128]{0:T(128)S(1)} %dynamic-update-slice), channel_id=1, replica_groups=mesh['pairs'=128,'tensor'=4] {'pairs'}, use_global_device_ids=true, to_apply=%add | all-reduce | flops 128 | bytes 1024
  326.3 1.6 compare_select_fusion
  327.9 175.8 %all-to-all-start = ((s32[128,1,2]{2,1,0:T(1,128)}), s32[128,1,2]{2,1,0:T(1,128)S(1)}, u32[]{:S(2)}, u32[]{:S(2)}) async-start(s32[128,1,2]{2,1,0:T(1,128)} %compare_select_fusion), calls=%async_computation | async-start | bytes 131072 | tf_op jit(solution)/shard_map/all_to_all | solution.py:87
  504.2 2.7 gather_fusion
  506.9 0.2 gather.7
  507.1 1.4 broadcast_select_fusion
  508.5 6.1 %all-to-all-done = s32[128,1,2]{2,1,0:T(1,128)S(1)} async-done(((s32[128,1,2]{2,1,0:T(1,128)}), s32[128,1,2]{2,1,0:T(1,128)S(1)}, u32[]{:S(2)}, u32[]{:S(2)}) %all-to-all-start) | async-done | bytes 1056 | tf_op jit(solution)/shard_map/all_to_all | solution.py:87
  514.6 7.5 %all-to-all-start.2 = ((bf16[128,2,1024]{2,1,0:T(2,128)(2,1)}), bf16[128,2,1024]{2,1,0:T(2,128)(2,1)S(1)}, u32[]{:S(2)}, u32[]{:S(2)}) async-start(bf16[128,2,1024]{2,1,0:T(2,128)(2,1)} %broadcast_select_fusion), calls=%async_computation.3 | async-start | bytes 1048576 | tf_op jit(solution)/shard_map/all_to_all | solution.py:86
  522.1 0.5 broadcast.219
  522.6 0.8 reduce.3
  523.5 19.2 %all-to-all-done.2 = bf16[128,2,1024]{2,1,0:T(2,128)(2,1)S(1)} async-done(((bf16[128,2,1024]{2,1,0:T(2,128)(2,1)}), bf16[128,2,1024]{2,1,0:T(2,128)(2,1)S(1)}, u32[]{:S(2)}, u32[]{:S(2)}) %all-to-all-start.2) | async-done | bytes 524320 | tf_op jit(solution)/shard_map/all_to_all | solution.py:86
  542.9 1.8 scatter_custom_fusion
  544.7 0.9 add_convert_fusion
  (36 shorter events, 1.5 us)
Async XLA Ops:
  11.7 18.6 %copy-start = (bf16[256,1024]{1,0:T(8,128)(2,1)S(1)}, bf16[256,1024]{1,0:T(8,128)(2,1)}, u32[]{:S(2)}) copy-start(bf16[256,1024]{1,0:T(8,128)(2,1)} %param.12) | copy-start | bytes 1572868
  11.7 18.8 %copy-start.1 = (bf16[256,1024]{1,0:T(8,128)(2,1)S(1)}, bf16[256,1024]{1,0:T(8,128)(2,1)}, u32[]{:S(2)}) copy-start(bf16[256,1024]{1,0:T(8,128)(2,1)} %param.10) | copy-start | bytes 1572868
  11.7 19.0 %copy-start.2 = (bf16[256,1024]{1,0:T(8,128)(2,1)S(1)}, bf16[256,1024]{1,0:T(8,128)(2,1)}, u32[]{:S(2)}) copy-start(bf16[256,1024]{1,0:T(8,128)(2,1)} %param.11) | copy-start | bytes 1572868
  11.7 19.2 %copy-start.4 = (s32[256]{0:T(256)S(1)}, s32[256]{0:T(256)}, u32[]{:S(2)}) copy-start(s32[256]{0:T(256)} %param.13) | copy-start | bytes 3076
  11.7 239.2 %all-to-all-start.1 = ((bf16[128,1024,32]{1,2,0:T(8,128)(2,1)}), bf16[128,1024,32]{1,2,0:T(8,128)(2,1)}, u32[]{:S(2)}, u32[]{:S(2)}) async-start(bf16[128,1024,32]{1,2,0:T(8,128)(2,1)} %stack.2), calls=%async_computation.1 | async-start | bytes 16777216 | tf_op jit(solution)/shard_map/all_to_all | solution.py:13
  30.2 474.1 %reduce-scatter.2.cloned.1.call-start = ((), (), s32[]{:S(2)}) async-start(), calls=%async_computation.4 | async-start | bytes 2621440 | tf_op jit(solution)/shard_map/reduce_scatter | solution.py:72
  258.1 286.5 %copy-start.3 = (bf16[192,1024]{1,0:T(8,128)(2,1)S(1)}, bf16[192,1024]{1,0:T(8,128)(2,1)}, u32[]{:S(2)}) copy-start(bf16[192,1024]{1,0:T(8,128)(2,1)} %param.15) | copy-start | bytes 1179652
  327.9 186.7 %all-to-all-start = ((s32[128,1,2]{2,1,0:T(1,128)}), s32[128,1,2]{2,1,0:T(1,128)S(1)}, u32[]{:S(2)}, u32[]{:S(2)}) async-start(s32[128,1,2]{2,1,0:T(1,128)} %compare_select_fusion), calls=%async_computation | async-start | bytes 131072 | tf_op jit(solution)/shard_map/all_to_all | solution.py:87
  514.6 28.1 %all-to-all-start.2 = ((bf16[128,2,1024]{2,1,0:T(2,128)(2,1)}), bf16[128,2,1024]{2,1,0:T(2,128)(2,1)S(1)}, u32[]{:S(2)}, u32[]{:S(2)}) async-start(bf16[128,2,1024]{2,1,0:T(2,128)(2,1)} %broadcast_select_fusion), calls=%async_computation.3 | async-start | bytes 1048576 | tf_op jit(solution)/shard_map/all_to_all | solution.py:86
Sparse Core Ops, SparseCore 0:
  258.3 75.7 reduce-scatter.1
